TPU v7x, 512 devices: a whole 4x4x16 slice. The times are simulated.
512 devices in a mesh: row: 32 (over z_lo, y), col: 16 (over z_hi, x, core).
Axes of the slice: x: 4, y: 4, z: 16 (z_hi: 2, z_lo: 8; z = z_hi * 8 + z_lo), core: 2. Of those that a mesh axis runs over, the one named last changes fastest.
Arguments:
- rhs: bfloat16 [32, 16, 64, 768], P('row', 'col'), may hold values from -6 to 6
- operator_blocks: bfloat16 [32, 16, 768, 768], P('row', 'col'), may hold values from -0.5 to 3.5
- local_solver: bfloat16 [32, 16, 768, 768], P('row', 'col'), may hold values from -0.1 to 0.6
- modes: bfloat16 [32, 16, 48, 768], P('row', 'col'), may hold values from -0.21875 to 0.21875
- coupling: bfloat16 [32, 16, 4, 128, 128], P('row', 'col'), may hold values from -0.25 to 0.25
- coarse_inverse: bfloat16 [16, 1536, 32, 768], P('col', None, 'row'), may hold values from -0.05 to 0.15
- send_block: int32 [32, 16, 8], P('row', 'col'), may hold values from 0 to 5
- slot_dir: int32 [32, 16, 4], P('row', 'col'), may hold values from -1 to 7, as said below
- slot_block: int32 [32, 16, 4], P('row', 'col'), may hold values from 0 to 5
Outputs:
- solution: float32 [32, 16, 64, 768], P('row', 'col')
Inputs may be any that keep to these rules, and one draw needn't show every extreme that they name: `slot_dir`: each subdomain lists 2 to 4 distinct directions toward subdomains inside the grid in its first slots; the remaining slots hold -1.
All inputs are finite; a program needn't handle non-finite values.
Results may differ from a plain program's by a relative error of at most 0.0033.
Values may be sent and summed in bfloat16 or wider, within the bound.
No kernel may reach another device: no remote copies, remote signals or barrier semaphores. Data moves between devices by JAX's collectives and lax.ppermute only.
A program may use at most 64 MiB of HBM per device.

v0:
```python
import jax
import jax.numpy as jnp
from jax import lax
from jax.sharding import PartitionSpec as P

ITERS = 6
OFFSETS = ((-1, -1), (-1, 0), (-1, 1), (0, -1), (0, 1), (1, -1), (1, 0), (1, 1))


def passed_along(block, axis, distance):
    devices = range(lax.axis_size(axis))
    route = [(i - distance, i) for i in devices if i - distance in devices]
    return lax.ppermute(block, axis, route)


def hop_rows(portion, steps):
    return passed_along(portion, "row", steps)


def hop_cols(portion, steps):
    return passed_along(portion, "col", steps)


def neighbour_pieces(outgoing):
    arrived = []
    for direction in range(8):
        shift_a, shift_b = OFFSETS[direction]
        portion = outgoing[7 - direction]
        if shift_a != 0:
            portion = hop_rows(portion, -shift_a)
        if shift_b != 0:
            portion = hop_cols(portion, -shift_b)
        arrived.append(portion)
    return jnp.stack(arrived, 0)


def on_device(
    rhs,
    operator_blocks,
    local_solver,
    modes,
    coupling,
    coarse_inverse,
    send_block,
    slot_dir,
    slot_block,
):
    highest = lax.Precision.HIGHEST
    columns = rhs.shape[2]
    unknowns = rhs.shape[3]
    block_size = coupling.shape[3]
    block_count = unknowns // block_size
    mode_count = modes.shape[2]
    piece_rows = mode_count * columns // 128
    rhs_full = rhs[0, 0].astype(jnp.float32)
    operator_matrix = operator_blocks[0, 0]
    solver_matrix = local_solver[0, 0]
    mode_basis = modes[0, 0]
    couplings = coupling[0, 0]
    coarse_tile = coarse_inverse[0, :, 0, :]
    send_onehot = (send_block[0, 0][:, None] == jnp.arange(block_count)[None, :]).astype(
        jnp.bfloat16
    )
    dir_onehot = (slot_dir[0, 0][:, None] == jnp.arange(8)[None, :]).astype(jnp.bfloat16)
    block_onehot = (slot_block[0, 0][:, None] == jnp.arange(block_count)[None, :]).astype(
        jnp.float32
    )
    col_index = lax.axis_index("col")

    def coarse_solve(rounded):
        restricted = lax.dot_general(
            mode_basis, rounded, (((1,), (1,)), ((), ())), preferred_element_type=jnp.float32
        )
        flat_piece = restricted.astype(jnp.bfloat16).reshape(piece_rows, 128)
        gathered = lax.all_gather(flat_piece, "row", axis=0, tiled=True).reshape(-1, columns)
        partial_sums = lax.dot_general(
            coarse_tile, gathered, (((0,), (0,)), ((), ())), preferred_element_type=jnp.float32
        )
        summed = lax.psum(partial_sums.reshape(-1, 128), "col")
        own_rows = lax.dynamic_slice_in_dim(summed, col_index * piece_rows, piece_rows, 0)
        return own_rows.reshape(mode_count, columns).astype(jnp.bfloat16)

    solution = jnp.zeros((columns, unknowns), jnp.float32)
    pending = None
    for iteration in range(ITERS):
        if iteration == 0:
            residual = rhs_full
        else:
            field_half = solution.astype(jnp.bfloat16)
            blocks = field_half.reshape(columns, block_count, block_size)
            outgoing = jnp.einsum(
                "ckn,ek->ecn", blocks, send_onehot, preferred_element_type=jnp.float32
            ).astype(jnp.bfloat16)
            incoming = neighbour_pieces(outgoing)
            chosen = jnp.einsum(
                "sd,dcn->scn", dir_onehot, incoming, preferred_element_type=jnp.float32
            ).astype(jnp.bfloat16)
            coupled = jnp.einsum(
                "scn,snm->scm", chosen, couplings, preferred_element_type=jnp.float32
            )
            placed = jnp.einsum("scm,sk->ckm", coupled, block_onehot, precision=highest).reshape(
                columns, unknowns
            )
            residual = rhs_full - (
                jnp.dot(field_half, operator_matrix, preferred_element_type=jnp.float32) + placed
            )
        rounded = residual.astype(jnp.bfloat16)
        update = jnp.dot(rounded, solver_matrix, preferred_element_type=jnp.float32)
        fresh = coarse_solve(rounded) if iteration + 1 < ITERS else None
        if pending is not None:
            update = update + lax.dot_general(
                pending, mode_basis, (((0,), (0,)), ((), ())), preferred_element_type=jnp.float32
            )
        solution = solution + update
        pending = fresh
    return solution[None, None]


def solution(mesh):
    in_specs = (
        P("row", "col", None, None),
        P("row", "col", None, None),
        P("row", "col", None, None),
        P("row", "col", None, None),
        P("row", "col", None, None, None),
        P("col", None, "row", None),
        P("row", "col", None),
        P("row", "col", None),
        P("row", "col", None),
    )
    out_specs = P("row", "col", None, None)
    return jax.shard_map(
        on_device, mesh=mesh, in_specs=in_specs, out_specs=out_specs, check_vma=False
    )
```

profile of v0, /device:TPU:23, one launch (start us, length us, event | category | flops | bytes accessed | tf_op | source)
XLA Modules:
  0.0 1464.4 jit_solution(8940192979941187941)
XLA Ops:
  17.5 100.3 %all_gather.15 = bf16[768,128]{1,0:T(8,128)(2,1)S(1)} all-gather(bf16[24,128]{1,0:T(8,128)(2,1)S(1)} %reshape.90), channel_id=1, replica_groups=mesh['row'=32,'col'=16] {'row'}, dimensions={0}, use_global_device_ids=true | all-gather | bytes 202752 | tf_op jit(solution)/shard_map/all_gather | solution.py:75
  118.7 23.7 %collective-permute-start.5 = (bf16[64,128]{1,0:T(8,128)(2,1)S(1)}, bf16[64,128]{1,0:T(8,128)(2,1)S(1)}, u32[]{:S(2)}, u32[]{:S(2)}) collective-permute-start(bf16[64,128]{1,0:T(8,128)(2,1)S(1)} %bitcast.406), channel_id=1, source_target_pairs={{0,1},{1,2},{2,3},{3,4},{4,5},{5,6},{6,7},{7,8},{8,9},{9,10},{10,1... | collective-permute-start | bytes 49160 | tf_op jit(solution)/shard_map/ppermute | solution.py:13
  144.4 124.1 %all-reduce.5 = bf16[384,128]{1,0:T(8,128)(2,1)S(1)} all-reduce(f32[384,128]{1,0:T(8,128)S(1)} %reshape.92), channel_id=1, replica_groups=mesh['row'=32,'col'=16] {'col'}, use_global_device_ids=true, to_apply=%region_0.0 | all-reduce | flops 49152 | bytes 294912 | tf_op jit(solution)/shard_map/psum | solution.py:79
  276.8 14.8 %collective-permute-start.1 = (bf16[64,128]{1,0:T(8,128)(2,1)S(1)}, bf16[64,128]{1,0:T(8,128)(2,1)S(1)}, u32[]{:S(2)}, u32[]{:S(2)}) collective-permute-start(bf16[64,128]{1,0:T(8,128)(2,1)S(1)} %collective-permute-done), channel_id=1, source_target_pairs={{0,1},{1,2},{2,3},{3,4},{4,5},{5,6},{6,7},{7,8},{8,9},{9,10},{10,1... | collective-permute-start | bytes 49160 | tf_op jit(solution)/shard_map/ppermute | solution.py:13
  293.5 14.5 collective-permute-start.8
  310.3 13.6 collective-permute-done.11
  359.6 96.8 %all_gather.16 = bf16[768,128]{1,0:T(8,128)(2,1)} all-gather(bf16[24,128]{1,0:T(8,128)(2,1)} %reshape.95), channel_id=1, replica_groups=mesh['row'=32,'col'=16] {'row'}, dimensions={0}, use_global_device_ids=true | all-gather | bytes 202752 | tf_op jit(solution)/shard_map/all_gather | solution.py:75
  470.4 28.7 %collective-permute-start.13 = (bf16[64,128]{1,0:T(8,128)(2,1)}, bf16[64,128]{1,0:T(8,128)(2,1)}, u32[]{:S(2)}, u32[]{:S(2)}) collective-permute-start(bf16[64,128]{1,0:T(8,128)(2,1)} %collective-permute-done.12), channel_id=1, source_target_pairs={{0,1},{1,2},{2,3},{3,4},{4,5},{5,6},{6,7},{7,8},{8,9},{9,10},{10,1... | collective-permute-start | bytes 49160 | tf_op jit(solution)/shard_map/ppermute | solution.py:13
  501.1 14.5 collective-permute-start.20
  541.5 95.9 %all_gather.17 = bf16[768,128]{1,0:T(8,128)(2,1)} all-gather(bf16[24,128]{1,0:T(8,128)(2,1)} %reshape.100), channel_id=1, replica_groups=mesh['row'=32,'col'=16] {'row'}, dimensions={0}, use_global_device_ids=true | all-gather | bytes 202752 | tf_op jit(solution)/shard_map/all_gather | solution.py:75
  645.1 141.5 %all-reduce.6 = (bf16[384,128]{1,0:T(8,128)(2,1)}, bf16[384,128]{1,0:T(8,128)(2,1)}) all-reduce(f32[384,128]{1,0:T(8,128)} %reshape.97, f32[384,128]{1,0:T(8,128)} %reshape.102), channel_id=1, replica_groups=mesh['row'=32,'col'=16] {'col'}, use_global_device_ids=true, to_apply=%region_1.0 | all-reduce | flops 98304 | bytes 589824 | tf_op jit(solution)/shard_map/psum | solution.py:79
  813.5 15.0 %collective-permute-start.29 = (bf16[64,128]{1,0:T(8,128)(2,1)S(1)}, bf16[64,128]{1,0:T(8,128)(2,1)S(1)}, u32[]{:S(2)}, u32[]{:S(2)}) collective-permute-start(bf16[64,128]{1,0:T(8,128)(2,1)S(1)} %bitcast.427), channel_id=1, source_target_pairs={{0,1},{1,2},{2,3},{3,4},{4,5},{5,6},{6,7},{7,8},{8,9},{9,10},{10,1... | collective-permute-start | bytes 49160 | tf_op jit(solution)/shard_map/ppermute | solution.py:13
  834.8 14.7 %collective-permute-start.25 = (bf16[64,128]{1,0:T(8,128)(2,1)}, bf16[64,128]{1,0:T(8,128)(2,1)}, u32[]{:S(2)}, u32[]{:S(2)}) collective-permute-start(bf16[64,128]{1,0:T(8,128)(2,1)} %collective-permute-done.24), channel_id=1, source_target_pairs={{0,1},{1,2},{2,3},{3,4},{4,5},{5,6},{6,7},{7,8},{8,9},{9,10},{10,1... | collective-permute-start | bytes 49160 | tf_op jit(solution)/shard_map/ppermute | solution.py:13
  851.5 14.5 collective-permute-start.32
  914.4 13.1 collective-permute-start.41
  929.4 97.0 %all_gather.18 = bf16[768,128]{1,0:T(8,128)(2,1)} all-gather(bf16[24,128]{1,0:T(8,128)(2,1)} %reshape.105), channel_id=1, replica_groups=mesh['row'=32,'col'=16] {'row'}, dimensions={0}, use_global_device_ids=true | all-gather | bytes 202752 | tf_op jit(solution)/shard_map/all_gather | solution.py:75
  1029.7 10.7 collective-permute-start.45
  1040.5 28.5 %collective-permute-start.37 = (bf16[64,128]{1,0:T(8,128)(2,1)}, bf16[64,128]{1,0:T(8,128)(2,1)}, u32[]{:S(2)}, u32[]{:S(2)}) collective-permute-start(bf16[64,128]{1,0:T(8,128)(2,1)} %collective-permute-done.36), channel_id=1, source_target_pairs={{0,1},{1,2},{2,3},{3,4},{4,5},{5,6},{6,7},{7,8},{8,9},{9,10},{10,1... | collective-permute-start | bytes 49160 | tf_op jit(solution)/shard_map/ppermute | solution.py:13
  1070.9 14.5 collective-permute-start.44
  1111.3 96.5 %all_gather.19 = bf16[768,128]{1,0:T(8,128)(2,1)} all-gather(bf16[24,128]{1,0:T(8,128)(2,1)} %reshape.110), channel_id=1, replica_groups=mesh['row'=32,'col'=16] {'row'}, dimensions={0}, use_global_device_ids=true | all-gather | bytes 202752 | tf_op jit(solution)/shard_map/all_gather | solution.py:75
  1215.5 141.9 %all-reduce.7 = (bf16[384,128]{1,0:T(8,128)(2,1)}, bf16[384,128]{1,0:T(8,128)(2,1)}) all-reduce(f32[384,128]{1,0:T(8,128)} %reshape.107, f32[384,128]{1,0:T(8,128)} %reshape.112), channel_id=1, replica_groups=mesh['row'=32,'col'=16] {'col'}, use_global_device_ids=true, to_apply=%region_3.0 | all-reduce | flops 98304 | bytes 589824 | tf_op jit(solution)/shard_map/psum | solution.py:79
  1384.5 15.0 %collective-permute-start.53 = (bf16[64,128]{1,0:T(8,128)(2,1)S(1)}, bf16[64,128]{1,0:T(8,128)(2,1)S(1)}, u32[]{:S(2)}, u32[]{:S(2)}) collective-permute-start(bf16[64,128]{1,0:T(8,128)(2,1)S(1)} %bitcast.428), channel_id=1, source_target_pairs={{0,1},{1,2},{2,3},{3,4},{4,5},{5,6},{6,7},{7,8},{8,9},{9,10},{10,1... | collective-permute-start | bytes 49160 | tf_op jit(solution)/shard_map/ppermute | solution.py:13
  1405.8 14.7 %collective-permute-start.49 = (bf16[64,128]{1,0:T(8,128)(2,1)}, bf16[64,128]{1,0:T(8,128)(2,1)}, u32[]{:S(2)}, u32[]{:S(2)}) collective-permute-start(bf16[64,128]{1,0:T(8,128)(2,1)} %collective-permute-done.48), channel_id=1, source_target_pairs={{0,1},{1,2},{2,3},{3,4},{4,5},{5,6},{6,7},{7,8},{8,9},{9,10},{10,1... | collective-permute-start | bytes 49160 | tf_op jit(solution)/shard_map/ppermute | solution.py:13
  1422.5 14.5 collective-permute-start.56
  (325 shorter events, 303.6 us)
Async XLA Ops:
  3.6 115.1 %collective-permute-start = (bf16[64,128]{1,0:T(8,128)(2,1)S(1)}, bf16[64,128]{1,0:T(8,128)(2,1)S(1)}, u32[]{:S(2)}, u32[]{:S(2)}) collective-permute-start(bf16[64,128]{1,0:T(8,128)(2,1)S(1)} %bitcast.426), channel_id=1, source_target_pairs={{0,16},{16,32},{32,48},{48,64},{64,80},{80,96},{96,112},{112,128},... | collective-permute-start | bytes 49160 | tf_op jit(solution)/shard_map/ppermute | solution.py:13
  6.5 135.9 %collective-permute-start.3 = (bf16[64,128]{1,0:T(8,128)(2,1)S(1)}, bf16[64,128]{1,0:T(8,128)(2,1)S(1)}, u32[]{:S(2)}, u32[]{:S(2)}) collective-permute-start(bf16[64,128]{1,0:T(8,128)(2,1)S(1)} %bitcast.424), channel_id=1, source_target_pairs={{0,16},{16,32},{32,48},{48,64},{64,80},{80,96},{96,112},{112,128},... | collective-permute-start | bytes 49160 | tf_op jit(solution)/shard_map/ppermute | solution.py:13
  9.8 258.8 %collective-permute-start.7 = (bf16[64,128]{1,0:T(8,128)(2,1)S(1)}, bf16[64,128]{1,0:T(8,128)(2,1)S(1)}, u32[]{:S(2)}, u32[]{:S(2)}) collective-permute-start(bf16[64,128]{1,0:T(8,128)(2,1)S(1)} %bitcast.404), channel_id=1, source_target_pairs={{16,0},{32,16},{48,32},{64,48},{80,64},{96,80},{112,96},{128,112},... | collective-permute-start | bytes 49160 | tf_op jit(solution)/shard_map/ppermute | solution.py:13
  11.9 264.9 %collective-permute-start.10 = (bf16[64,128]{1,0:T(8,128)(2,1)S(1)}, bf16[64,128]{1,0:T(8,128)(2,1)S(1)}, u32[]{:S(2)}, u32[]{:S(2)}) collective-permute-start(bf16[64,128]{1,0:T(8,128)(2,1)S(1)} %bitcast.403), channel_id=1, source_target_pairs={{16,0},{32,16},{48,32},{64,48},{80,64},{96,80},{112,96},{128,112},... | collective-permute-start | bytes 49160 | tf_op jit(solution)/shard_map/ppermute | solution.py:13
  14.3 277.3 %collective-permute-start.2 = (bf16[64,128]{1,0:T(8,128)(2,1)S(1)}, bf16[64,128]{1,0:T(8,128)(2,1)S(1)}, u32[]{:S(2)}, u32[]{:S(2)}) collective-permute-start(bf16[64,128]{1,0:T(8,128)(2,1)S(1)} %bitcast.401), channel_id=1, source_target_pairs={{0,16},{16,32},{32,48},{48,64},{64,80},{80,96},{96,112},{112,128},... | collective-permute-start | bytes 49160 | tf_op jit(solution)/shard_map/ppermute | solution.py:13
  118.7 174.8 %collective-permute-start.5 = (bf16[64,128]{1,0:T(8,128)(2,1)S(1)}, bf16[64,128]{1,0:T(8,128)(2,1)S(1)}, u32[]{:S(2)}, u32[]{:S(2)}) collective-permute-start(bf16[64,128]{1,0:T(8,128)(2,1)S(1)} %bitcast.406), channel_id=1, source_target_pairs={{0,1},{1,2},{2,3},{3,4},{4,5},{5,6},{6,7},{7,8},{8,9},{9,10},{10,1... | collective-permute-start | bytes 49160 | tf_op jit(solution)/shard_map/ppermute | solution.py:13
  142.5 165.5 %collective-permute-start.6 = (bf16[64,128]{1,0:T(8,128)(2,1)S(1)}, bf16[64,128]{1,0:T(8,128)(2,1)S(1)}, u32[]{:S(2)}, u32[]{:S(2)}) collective-permute-start(bf16[64,128]{1,0:T(8,128)(2,1)S(1)} %bitcast.402), channel_id=1, source_target_pairs={{1,0},{2,1},{3,2},{4,3},{5,4},{6,5},{7,6},{8,7},{9,8},{10,9},{11,1... | collective-permute-start | bytes 49160 | tf_op jit(solution)/shard_map/ppermute | solution.py:13
  268.5 41.6 %collective-permute-start.9 = (bf16[64,128]{1,0:T(8,128)(2,1)S(1)}, bf16[64,128]{1,0:T(8,128)(2,1)S(1)}, u32[]{:S(2)}, u32[]{:S(2)}) collective-permute-start(bf16[64,128]{1,0:T(8,128)(2,1)S(1)} %bitcast.408), channel_id=1, source_target_pairs={{16,0},{32,16},{48,32},{64,48},{80,64},{96,80},{112,96},{128,112},... | collective-permute-start | bytes 49160 | tf_op jit(solution)/shard_map/ppermute | solution.py:13
  340.2 119.5 %collective-permute-start.19 = (bf16[64,128]{1,0:T(8,128)(2,1)}, bf16[64,128]{1,0:T(8,128)(2,1)}, u32[]{:S(2)}, u32[]{:S(2)}) collective-permute-start(bf16[64,128]{1,0:T(8,128)(2,1)} %bitcast.380), channel_id=1, source_target_pairs={{16,0},{32,16},{48,32},{64,48},{80,64},{96,80},{112,96},{128,112},... | collective-permute-start | bytes 49160 | tf_op jit(solution)/shard_map/ppermute | solution.py:13
  346.5 123.8 %collective-permute-start.22 = (bf16[64,128]{1,0:T(8,128)(2,1)}, bf16[64,128]{1,0:T(8,128)(2,1)}, u32[]{:S(2)}, u32[]{:S(2)}) collective-permute-start(bf16[64,128]{1,0:T(8,128)(2,1)} %bitcast.378), channel_id=1, source_target_pairs={{16,0},{32,16},{48,32},{64,48},{80,64},{96,80},{112,96},{128,112},... | collective-permute-start | bytes 49160 | tf_op jit(solution)/shard_map/ppermute | solution.py:13
  351.1 148.0 %collective-permute-start.14 = (bf16[64,128]{1,0:T(8,128)(2,1)}, bf16[64,128]{1,0:T(8,128)(2,1)}, u32[]{:S(2)}, u32[]{:S(2)}) collective-permute-start(bf16[64,128]{1,0:T(8,128)(2,1)} %bitcast.384), channel_id=1, source_target_pairs={{0,16},{16,32},{32,48},{48,64},{64,80},{80,96},{96,112},{112,128},... | collective-permute-start | bytes 49160 | tf_op jit(solution)/shard_map/ppermute | solution.py:13
  354.9 146.2 %collective-permute-start.17 = (bf16[64,128]{1,0:T(8,128)(2,1)}, bf16[64,128]{1,0:T(8,128)(2,1)S(1)}, u32[]{:S(2)}, u32[]{:S(2)}) collective-permute-start(bf16[64,128]{1,0:T(8,128)(2,1)} %bitcast.419), channel_id=1, source_target_pairs={{0,1},{1,2},{2,3},{3,4},{4,5},{5,6},{6,7},{7,8},{8,9},{9,10},{10,1... | collective-permute-start | bytes 49160 | tf_op jit(solution)/shard_map/ppermute | solution.py:13
  357.7 157.9 %collective-permute-start.18 = (bf16[64,128]{1,0:T(8,128)(2,1)}, bf16[64,128]{1,0:T(8,128)(2,1)}, u32[]{:S(2)}, u32[]{:S(2)}) collective-permute-start(bf16[64,128]{1,0:T(8,128)(2,1)} %bitcast.413), channel_id=1, source_target_pairs={{1,0},{2,1},{3,2},{4,3},{5,4},{6,5},{7,6},{8,7},{9,8},{10,9},{11,1... | collective-permute-start | bytes 49160 | tf_op jit(solution)/shard_map/ppermute | solution.py:13
  459.7 67.0 %collective-permute-start.21 = (bf16[64,128]{1,0:T(8,128)(2,1)}, bf16[64,128]{1,0:T(8,128)(2,1)}, u32[]{:S(2)}, u32[]{:S(2)}) collective-permute-start(bf16[64,128]{1,0:T(8,128)(2,1)} %bitcast.416), channel_id=1, source_target_pairs={{16,0},{32,16},{48,32},{64,48},{80,64},{96,80},{112,96},{128,112},... | collective-permute-start | bytes 49160 | tf_op jit(solution)/shard_map/ppermute | solution.py:13
  470.4 57.6 %collective-permute-start.13 = (bf16[64,128]{1,0:T(8,128)(2,1)}, bf16[64,128]{1,0:T(8,128)(2,1)}, u32[]{:S(2)}, u32[]{:S(2)}) collective-permute-start(bf16[64,128]{1,0:T(8,128)(2,1)} %collective-permute-done.12), channel_id=1, source_target_pairs={{0,1},{1,2},{2,3},{3,4},{4,5},{5,6},{6,7},{7,8},{8,9},{9,10},{10,1... | collective-permute-start | bytes 49160 | tf_op jit(solution)/shard_map/ppermute | solution.py:13
  831.1 43.1 %collective-permute-start.33 = (bf16[64,128]{1,0:T(8,128)(2,1)}, bf16[64,128]{1,0:T(8,128)(2,1)}, u32[]{:S(2)}, u32[]{:S(2)}) collective-permute-start(bf16[64,128]{1,0:T(8,128)(2,1)} %bitcast.371), channel_id=1, source_target_pairs={{16,0},{32,16},{48,32},{64,48},{80,64},{96,80},{112,96},{128,112},... | collective-permute-start | bytes 49160 | tf_op jit(solution)/shard_map/ppermute | solution.py:13
  903.0 126.6 %collective-permute-start.43 = (bf16[64,128]{1,0:T(8,128)(2,1)}, bf16[64,128]{1,0:T(8,128)(2,1)}, u32[]{:S(2)}, u32[]{:S(2)}) collective-permute-start(bf16[64,128]{1,0:T(8,128)(2,1)} %bitcast.364), channel_id=1, source_target_pairs={{16,0},{32,16},{48,32},{64,48},{80,64},{96,80},{112,96},{128,112},... | collective-permute-start | bytes 49160 | tf_op jit(solution)/shard_map/ppermute | solution.py:13
  906.0 134.4 %collective-permute-start.46 = (bf16[64,128]{1,0:T(8,128)(2,1)}, bf16[64,128]{1,0:T(8,128)(2,1)}, u32[]{:S(2)}, u32[]{:S(2)}) collective-permute-start(bf16[64,128]{1,0:T(8,128)(2,1)} %bitcast.362), channel_id=1, source_target_pairs={{16,0},{32,16},{48,32},{64,48},{80,64},{96,80},{112,96},{128,112},... | collective-permute-start | bytes 49160 | tf_op jit(solution)/shard_map/ppermute | solution.py:13
  910.6 158.4 %collective-permute-start.38 = (bf16[64,128]{1,0:T(8,128)(2,1)}, bf16[64,128]{1,0:T(8,128)(2,1)}, u32[]{:S(2)}, u32[]{:S(2)}) collective-permute-start(bf16[64,128]{1,0:T(8,128)(2,1)} %bitcast.368), channel_id=1, source_target_pairs={{0,16},{16,32},{32,48},{48,64},{64,80},{80,96},{96,112},{112,128},... | collective-permute-start | bytes 49160 | tf_op jit(solution)/shard_map/ppermute | solution.py:13
  914.4 156.5 %collective-permute-start.41 = (bf16[64,128]{1,0:T(8,128)(2,1)}, bf16[64,128]{1,0:T(8,128)(2,1)S(1)}, u32[]{:S(2)}, u32[]{:S(2)}) collective-permute-start(bf16[64,128]{1,0:T(8,128)(2,1)} %bitcast.421), channel_id=1, source_target_pairs={{0,1},{1,2},{2,3},{3,4},{4,5},{5,6},{6,7},{7,8},{8,9},{9,10},{10,1... | collective-permute-start | bytes 49160 | tf_op jit(solution)/shard_map/ppermute | solution.py:13
  927.5 157.9 %collective-permute-start.42 = (bf16[64,128]{1,0:T(8,128)(2,1)}, bf16[64,128]{1,0:T(8,128)(2,1)}, u32[]{:S(2)}, u32[]{:S(2)}) collective-permute-start(bf16[64,128]{1,0:T(8,128)(2,1)} %bitcast.414), channel_id=1, source_target_pairs={{1,0},{2,1},{3,2},{4,3},{5,4},{6,5},{7,6},{8,7},{9,8},{10,9},{11,1... | collective-permute-start | bytes 49160 | tf_op jit(solution)/shard_map/ppermute | solution.py:13
  1029.7 66.8 %collective-permute-start.45 = (bf16[64,128]{1,0:T(8,128)(2,1)}, bf16[64,128]{1,0:T(8,128)(2,1)}, u32[]{:S(2)}, u32[]{:S(2)}) collective-permute-start(bf16[64,128]{1,0:T(8,128)(2,1)} %bitcast.417), channel_id=1, source_target_pairs={{16,0},{32,16},{48,32},{64,48},{80,64},{96,80},{112,96},{128,112},... | collective-permute-start | bytes 49160 | tf_op jit(solution)/shard_map/ppermute | solution.py:13
  1040.5 57.4 %collective-permute-start.37 = (bf16[64,128]{1,0:T(8,128)(2,1)}, bf16[64,128]{1,0:T(8,128)(2,1)}, u32[]{:S(2)}, u32[]{:S(2)}) collective-permute-start(bf16[64,128]{1,0:T(8,128)(2,1)} %collective-permute-done.36), channel_id=1, source_target_pairs={{0,1},{1,2},{2,3},{3,4},{4,5},{5,6},{6,7},{7,8},{8,9},{9,10},{10,1... | collective-permute-start | bytes 49160 | tf_op jit(solution)/shard_map/ppermute | solution.py:13
  1402.1 41.7 %collective-permute-start.57 = (bf16[64,128]{1,0:T(8,128)(2,1)}, bf16[64,128]{1,0:T(8,128)(2,1)}, u32[]{:S(2)}, u32[]{:S(2)}) collective-permute-start(bf16[64,128]{1,0:T(8,128)(2,1)} %bitcast.355), channel_id=1, source_target_pairs={{16,0},{32,16},{48,32},{64,48},{80,64},{96,80},{112,96},{128,112},... | collective-permute-start | bytes 49160 | tf_op jit(solution)/shard_map/ppermute | solution.py:13
  (62 other events, 1878.5 us)
where the time goes:
time: 1470 us; the launch traced here: 1460 us
  blocking collectives  894 us (61%)
  starting transfers between devices  391 us (27%)
  local copies, waits for them, and re-layouts  105 us (7%)
  matrix products  52.9 us (4%)
  waiting for transfers between devices  20.2 us (1%)
    all_gather x5, blocking collectives, coarse_solve(): lax.all_gather(flat_piece, 'row', axis=0, tiled=True).reshape(-1, columns)  487 us
    psum x3, blocking collectives, coarse_solve(): summed = lax.psum(partial_sums.reshape(-1, 128), 'col')  408 us
    ppermute x60, starting transfers between devices, passed_along(): return lax.ppermute(block, axis, route)  391 us
    another operation x45, local copies, waits for them, and re-layouts, neighbour_pieces(): return jnp.stack(arrived, 0)  50 us
  transfers between devices with their start and end apart: 60, of which 3 were waited for; matrix products, arithmetic and copies ran while one was open for 5% of the time, Pallas kernels for 0%

commit v1 on v0

--- a/solution.py
+++ b/solution.py
@@ -76,7 +76,7 @@
         partial_sums = lax.dot_general(
             coarse_tile, gathered, (((0,), (0,)), ((), ())), preferred_element_type=jnp.float32
         )
-        summed = lax.psum(partial_sums.reshape(-1, 128), "col")
+        summed = jnp.sum(lax.all_gather(partial_sums.reshape(-1, 128), "col"), axis=0)
         own_rows = lax.dynamic_slice_in_dim(summed, col_index * piece_rows, piece_rows, 0)
         return own_rows.reshape(mode_count, columns).astype(jnp.bfloat16)
 

time: 1470 us -> 1200 us (0.82)
  the two profiles are of different devices: /device:TPU:23 before, /device:TPU:448 now
where the time goes in v1:
time: 1200 us
  blocking collectives  511 us (43%)
  starting transfers between devices  380 us (32%)
  waiting for transfers between devices  127 us (11%)
  local copies, waits for them, and re-layouts  91.6 us (8%)
  matrix products  59.6 us (5%)
  between operations  14.7 us (1%)
  other arithmetic  13.5 us (1%)
    all_gather x5, blocking collectives, coarse_solve(): lax.all_gather(flat_piece, 'row', axis=0, tiled=True).reshape(-1, columns)  511 us
    ppermute x60, starting transfers between devices, passed_along(): return lax.ppermute(block, axis, route)  379 us
    all_gather x5, waiting for transfers between devices, coarse_solve(): lax.all_gather(partial_sums.reshape(-1, 128), 'col')  127 us
    another operation x45, local copies, waits for them, and re-layouts, neighbour_pieces(): return jnp.stack(arrived, 0)  40.7 us
  transfers between devices with their start and end apart: 65, of which 1 were waited for; matrix products, arithmetic and copies ran while one was open for 11% of the time, Pallas kernels for 0%

profile of v1, /device:TPU:448, one launch (start us, length us, event | category | flops | bytes accessed | tf_op | source)
XLA Modules:
  0.0 1197.5 jit_solution(12922961795575022660)
XLA Ops:
  7.9 83.1 %all_gather.30 = bf16[768,128]{1,0:T(8,128)(2,1)S(1)} all-gather(bf16[24,128]{1,0:T(8,128)(2,1)S(1)} %reshape.75), channel_id=1, replica_groups=mesh['row'=32,'col'=16] {'row'}, dimensions={0}, use_global_device_ids=true | all-gather | bytes 202752 | tf_op jit(solution)/shard_map/all_gather | solution.py:75
  125.8 14.5 %collective-permute-start.6 = (bf16[64,128]{1,0:T(8,128)(2,1)S(1)}, bf16[64,128]{1,0:T(8,128)(2,1)S(1)}, u32[]{:S(2)}, u32[]{:S(2)}) collective-permute-start(bf16[64,128]{1,0:T(8,128)(2,1)S(1)} %bitcast.428), channel_id=1, source_target_pairs={{1,0},{2,1},{3,2},{4,3},{5,4},{6,5},{7,6},{8,7},{9,8},{10,9},{11,1... | collective-permute-start | bytes 49160 | tf_op jit(solution)/shard_map/ppermute | solution.py:13
  148.1 14.5 %collective-permute-start.4 = (bf16[64,128]{1,0:T(8,128)(2,1)S(1)}, bf16[64,128]{1,0:T(8,128)(2,1)S(1)}, u32[]{:S(2)}, u32[]{:S(2)}) collective-permute-start(bf16[64,128]{1,0:T(8,128)(2,1)S(1)} %collective-permute-done.3), channel_id=1, source_target_pairs={{1,0},{2,1},{3,2},{4,3},{5,4},{6,5},{7,6},{8,7},{9,8},{10,9},{11,1... | collective-permute-start | bytes 49160 | tf_op jit(solution)/shard_map/ppermute | solution.py:13
  164.5 14.5 %collective-permute-start.11 = (bf16[64,128]{1,0:T(8,128)(2,1)S(1)}, bf16[64,128]{1,0:T(8,128)(2,1)S(1)}, u32[]{:S(2)}, u32[]{:S(2)}) collective-permute-start(bf16[64,128]{1,0:T(8,128)(2,1)S(1)} %collective-permute-done.10), channel_id=1, source_target_pairs={{1,0},{2,1},{3,2},{4,3},{5,4},{6,5},{7,6},{8,7},{9,8},{10,9},{11,1... | collective-permute-start | bytes 49160 | tf_op jit(solution)/shard_map/ppermute | solution.py:13
  191.8 106.4 %all_gather.32 = bf16[768,128]{1,0:T(8,128)(2,1)} all-gather(bf16[24,128]{1,0:T(8,128)(2,1)} %reshape.79), channel_id=1, replica_groups=mesh['row'=32,'col'=16] {'row'}, dimensions={0}, use_global_device_ids=true | all-gather | bytes 202752 | tf_op jit(solution)/shard_map/all_gather | solution.py:75
  330.2 10.3 collective-permute-start.15
  342.4 14.5 %collective-permute-start.18 = (bf16[64,128]{1,0:T(8,128)(2,1)S(1)}, bf16[64,128]{1,0:T(8,128)(2,1)S(1)}, u32[]{:S(2)}, u32[]{:S(2)}) collective-permute-start(bf16[64,128]{1,0:T(8,128)(2,1)S(1)} %bitcast.429), channel_id=1, source_target_pairs={{1,0},{2,1},{3,2},{4,3},{5,4},{6,5},{7,6},{8,7},{9,8},{10,9},{11,1... | collective-permute-start | bytes 49160 | tf_op jit(solution)/shard_map/ppermute | solution.py:13
  364.7 14.5 %collective-permute-start.16 = (bf16[64,128]{1,0:T(8,128)(2,1)S(1)}, bf16[64,128]{1,0:T(8,128)(2,1)S(1)}, u32[]{:S(2)}, u32[]{:S(2)}) collective-permute-start(bf16[64,128]{1,0:T(8,128)(2,1)S(1)} %collective-permute-done.15), channel_id=1, source_target_pairs={{1,0},{2,1},{3,2},{4,3},{5,4},{6,5},{7,6},{8,7},{9,8},{10,9},{11,1... | collective-permute-start | bytes 49160 | tf_op jit(solution)/shard_map/ppermute | solution.py:13
  381.1 14.5 %collective-permute-start.23 = (bf16[64,128]{1,0:T(8,128)(2,1)S(1)}, bf16[64,128]{1,0:T(8,128)(2,1)S(1)}, u32[]{:S(2)}, u32[]{:S(2)}) collective-permute-start(bf16[64,128]{1,0:T(8,128)(2,1)S(1)} %collective-permute-done.22), channel_id=1, source_target_pairs={{1,0},{2,1},{3,2},{4,3},{5,4},{6,5},{7,6},{8,7},{9,8},{10,9},{11,1... | collective-permute-start | bytes 49160 | tf_op jit(solution)/shard_map/ppermute | solution.py:13
  408.4 107.2 %all_gather.34 = bf16[768,128]{1,0:T(8,128)(2,1)} all-gather(bf16[24,128]{1,0:T(8,128)(2,1)} %reshape.83), channel_id=1, replica_groups=mesh['row'=32,'col'=16] {'row'}, dimensions={0}, use_global_device_ids=true | all-gather | bytes 202752 | tf_op jit(solution)/shard_map/all_gather | solution.py:75
  547.6 10.3 collective-permute-start.27
  559.9 14.5 %collective-permute-start.30 = (bf16[64,128]{1,0:T(8,128)(2,1)S(1)}, bf16[64,128]{1,0:T(8,128)(2,1)S(1)}, u32[]{:S(2)}, u32[]{:S(2)}) collective-permute-start(bf16[64,128]{1,0:T(8,128)(2,1)S(1)} %bitcast.430), channel_id=1, source_target_pairs={{1,0},{2,1},{3,2},{4,3},{5,4},{6,5},{7,6},{8,7},{9,8},{10,9},{11,1... | collective-permute-start | bytes 49160 | tf_op jit(solution)/shard_map/ppermute | solution.py:13
  582.1 14.5 %collective-permute-start.28 = (bf16[64,128]{1,0:T(8,128)(2,1)S(1)}, bf16[64,128]{1,0:T(8,128)(2,1)S(1)}, u32[]{:S(2)}, u32[]{:S(2)}) collective-permute-start(bf16[64,128]{1,0:T(8,128)(2,1)S(1)} %collective-permute-done.27), channel_id=1, source_target_pairs={{1,0},{2,1},{3,2},{4,3},{5,4},{6,5},{7,6},{8,7},{9,8},{10,9},{11,1... | collective-permute-start | bytes 49160 | tf_op jit(solution)/shard_map/ppermute | solution.py:13
  598.6 14.6 %collective-permute-start.35 = (bf16[64,128]{1,0:T(8,128)(2,1)S(1)}, bf16[64,128]{1,0:T(8,128)(2,1)S(1)}, u32[]{:S(2)}, u32[]{:S(2)}) collective-permute-start(bf16[64,128]{1,0:T(8,128)(2,1)S(1)} %collective-permute-done.34), channel_id=1, source_target_pairs={{1,0},{2,1},{3,2},{4,3},{5,4},{6,5},{7,6},{8,7},{9,8},{10,9},{11,1... | collective-permute-start | bytes 49160 | tf_op jit(solution)/shard_map/ppermute | solution.py:13
  626.0 107.3 %all_gather.36 = bf16[768,128]{1,0:T(8,128)(2,1)} all-gather(bf16[24,128]{1,0:T(8,128)(2,1)} %reshape.87), channel_id=1, replica_groups=mesh['row'=32,'col'=16] {'row'}, dimensions={0}, use_global_device_ids=true | all-gather | bytes 202752 | tf_op jit(solution)/shard_map/all_gather | solution.py:75
  765.3 10.3 collective-permute-start.39
  777.5 14.5 %collective-permute-start.42 = (bf16[64,128]{1,0:T(8,128)(2,1)S(1)}, bf16[64,128]{1,0:T(8,128)(2,1)S(1)}, u32[]{:S(2)}, u32[]{:S(2)}) collective-permute-start(bf16[64,128]{1,0:T(8,128)(2,1)S(1)} %bitcast.431), channel_id=1, source_target_pairs={{1,0},{2,1},{3,2},{4,3},{5,4},{6,5},{7,6},{8,7},{9,8},{10,9},{11,1... | collective-permute-start | bytes 49160 | tf_op jit(solution)/shard_map/ppermute | solution.py:13
  799.8 14.5 %collective-permute-start.40 = (bf16[64,128]{1,0:T(8,128)(2,1)S(1)}, bf16[64,128]{1,0:T(8,128)(2,1)S(1)}, u32[]{:S(2)}, u32[]{:S(2)}) collective-permute-start(bf16[64,128]{1,0:T(8,128)(2,1)S(1)} %collective-permute-done.39), channel_id=1, source_target_pairs={{1,0},{2,1},{3,2},{4,3},{5,4},{6,5},{7,6},{8,7},{9,8},{10,9},{11,1... | collective-permute-start | bytes 49160 | tf_op jit(solution)/shard_map/ppermute | solution.py:13
  816.2 14.5 %collective-permute-start.47 = (bf16[64,128]{1,0:T(8,128)(2,1)S(1)}, bf16[64,128]{1,0:T(8,128)(2,1)S(1)}, u32[]{:S(2)}, u32[]{:S(2)}) collective-permute-start(bf16[64,128]{1,0:T(8,128)(2,1)S(1)} %collective-permute-done.46), channel_id=1, source_target_pairs={{1,0},{2,1},{3,2},{4,3},{5,4},{6,5},{7,6},{8,7},{9,8},{10,9},{11,1... | collective-permute-start | bytes 49160 | tf_op jit(solution)/shard_map/ppermute | solution.py:13
  843.5 107.2 %all_gather.38 = bf16[768,128]{1,0:T(8,128)(2,1)} all-gather(bf16[24,128]{1,0:T(8,128)(2,1)} %reshape.91), channel_id=1, replica_groups=mesh['row'=32,'col'=16] {'row'}, dimensions={0}, use_global_device_ids=true | all-gather | bytes 202752 | tf_op jit(solution)/shard_map/all_gather | solution.py:75
  963.1 126.9 %all-gather.14.cloned.1.call-done = f32[16,384,128]{2,1,0:T(8,128)} async-done(((f32[1,384,128]{2,1,0:T(8,128)}), f32[16,384,128]{2,1,0:T(8,128)}) %all-gather.14.cloned.1.call-update) | async-done | bytes 3145744 | tf_op jit(solution)/shard_map/all_gather | solution.py:79
  1111.8 14.5 %collective-permute-start.54 = (bf16[64,128]{1,0:T(8,128)(2,1)S(1)}, bf16[64,128]{1,0:T(8,128)(2,1)S(1)}, u32[]{:S(2)}, u32[]{:S(2)}) collective-permute-start(bf16[64,128]{1,0:T(8,128)(2,1)S(1)} %bitcast.432), channel_id=1, source_target_pairs={{1,0},{2,1},{3,2},{4,3},{5,4},{6,5},{7,6},{8,7},{9,8},{10,9},{11,1... | collective-permute-start | bytes 49160 | tf_op jit(solution)/shard_map/ppermute | solution.py:13
  1138.6 14.5 %collective-permute-start.52 = (bf16[64,128]{1,0:T(8,128)(2,1)}, bf16[64,128]{1,0:T(8,128)(2,1)}, u32[]{:S(2)}, u32[]{:S(2)}) collective-permute-start(bf16[64,128]{1,0:T(8,128)(2,1)} %collective-permute-done.51), channel_id=1, source_target_pairs={{1,0},{2,1},{3,2},{4,3},{5,4},{6,5},{7,6},{8,7},{9,8},{10,9},{11,1... | collective-permute-start | bytes 49160 | tf_op jit(solution)/shard_map/ppermute | solution.py:13
  1155.0 14.5 %collective-permute-start.59 = (bf16[64,128]{1,0:T(8,128)(2,1)}, bf16[64,128]{1,0:T(8,128)(2,1)}, u32[]{:S(2)}, u32[]{:S(2)}) collective-permute-start(bf16[64,128]{1,0:T(8,128)(2,1)} %collective-permute-done.58), channel_id=1, source_target_pairs={{1,0},{2,1},{3,2},{4,3},{5,4},{6,5},{7,6},{8,7},{9,8},{10,9},{11,1... | collective-permute-start | bytes 49160 | tf_op jit(solution)/shard_map/ppermute | solution.py:13
  (336 shorter events, 296.7 us)
Async XLA Ops:
  6.5 301.3 %all-gather.6.cloned.1.call-start = ((), (), s32[]{:S(2)}) async-start(), calls=%async_computation | async-start | bytes 3342336 | tf_op jit(solution)/shard_map/all_gather | solution.py:79
  96.1 429.3 %all-gather.8.cloned.1.call-start = ((), (), s32[]{:S(2)}) async-start(), calls=%async_computation.1 | async-start | bytes 3342336 | tf_op jit(solution)/shard_map/all_gather | solution.py:79
  101.2 39.2 %collective-permute-start = (bf16[64,128]{1,0:T(8,128)(2,1)S(1)}, bf16[64,128]{1,0:T(8,128)(2,1)S(1)}, u32[]{:S(2)}, u32[]{:S(2)}) collective-permute-start(bf16[64,128]{1,0:T(8,128)(2,1)S(1)} %bitcast.468), channel_id=1, source_target_pairs={{0,16},{16,32},{32,48},{48,64},{64,80},{80,96},{96,112},{112,128},... | collective-permute-start | bytes 49160 | tf_op jit(solution)/shard_map/ppermute | solution.py:13
  144.2 36.7 %collective-permute-start.9 = (bf16[64,128]{1,0:T(8,128)(2,1)S(1)}, bf16[64,128]{1,0:T(8,128)(2,1)S(1)}, u32[]{:S(2)}, u32[]{:S(2)}) collective-permute-start(bf16[64,128]{1,0:T(8,128)(2,1)S(1)} %bitcast.419), channel_id=1, source_target_pairs={{16,0},{32,16},{48,32},{64,48},{80,64},{96,80},{112,96},{128,112},... | collective-permute-start | bytes 49160 | tf_op jit(solution)/shard_map/ppermute | solution.py:13
  146.2 35.4 %collective-permute-start.1 = (bf16[64,128]{1,0:T(8,128)(2,1)S(1)}, bf16[64,128]{1,0:T(8,128)(2,1)S(1)}, u32[]{:S(2)}, u32[]{:S(2)}) collective-permute-start(bf16[64,128]{1,0:T(8,128)(2,1)S(1)} %collective-permute-done), channel_id=1, source_target_pairs={{0,1},{1,2},{2,3},{3,4},{4,5},{5,6},{6,7},{7,8},{8,9},{9,10},{10,1... | collective-permute-start | bytes 49160 | tf_op jit(solution)/shard_map/ppermute | solution.py:13
  148.1 34.1 %collective-permute-start.4 = (bf16[64,128]{1,0:T(8,128)(2,1)S(1)}, bf16[64,128]{1,0:T(8,128)(2,1)S(1)}, u32[]{:S(2)}, u32[]{:S(2)}) collective-permute-start(bf16[64,128]{1,0:T(8,128)(2,1)S(1)} %collective-permute-done.3), channel_id=1, source_target_pairs={{1,0},{2,1},{3,2},{4,3},{5,4},{6,5},{7,6},{8,7},{9,8},{10,9},{11,1... | collective-permute-start | bytes 49160 | tf_op jit(solution)/shard_map/ppermute | solution.py:13
  305.9 437.1 %all-gather.10.cloned.1.call-start = ((), (), s32[]{:S(2)}) async-start(), calls=%async_computation.2 | async-start | bytes 3342336 | tf_op jit(solution)/shard_map/all_gather | solution.py:79
  317.7 39.2 %collective-permute-start.12 = (bf16[64,128]{1,0:T(8,128)(2,1)S(1)}, bf16[64,128]{1,0:T(8,128)(2,1)S(1)}, u32[]{:S(2)}, u32[]{:S(2)}) collective-permute-start(bf16[64,128]{1,0:T(8,128)(2,1)S(1)} %bitcast.469), channel_id=1, source_target_pairs={{0,16},{16,32},{32,48},{48,64},{64,80},{80,96},{96,112},{112,128},... | collective-permute-start | bytes 49160 | tf_op jit(solution)/shard_map/ppermute | solution.py:13
  360.8 36.7 %collective-permute-start.21 = (bf16[64,128]{1,0:T(8,128)(2,1)S(1)}, bf16[64,128]{1,0:T(8,128)(2,1)S(1)}, u32[]{:S(2)}, u32[]{:S(2)}) collective-permute-start(bf16[64,128]{1,0:T(8,128)(2,1)S(1)} %bitcast.420), channel_id=1, source_target_pairs={{16,0},{32,16},{48,32},{64,48},{80,64},{96,80},{112,96},{128,112},... | collective-permute-start | bytes 49160 | tf_op jit(solution)/shard_map/ppermute | solution.py:13
  362.8 35.4 %collective-permute-start.13 = (bf16[64,128]{1,0:T(8,128)(2,1)S(1)}, bf16[64,128]{1,0:T(8,128)(2,1)S(1)}, u32[]{:S(2)}, u32[]{:S(2)}) collective-permute-start(bf16[64,128]{1,0:T(8,128)(2,1)S(1)} %collective-permute-done.12), channel_id=1, source_target_pairs={{0,1},{1,2},{2,3},{3,4},{4,5},{5,6},{6,7},{7,8},{8,9},{9,10},{10,1... | collective-permute-start | bytes 49160 | tf_op jit(solution)/shard_map/ppermute | solution.py:13
  364.7 34.1 %collective-permute-start.16 = (bf16[64,128]{1,0:T(8,128)(2,1)S(1)}, bf16[64,128]{1,0:T(8,128)(2,1)S(1)}, u32[]{:S(2)}, u32[]{:S(2)}) collective-permute-start(bf16[64,128]{1,0:T(8,128)(2,1)S(1)} %collective-permute-done.15), channel_id=1, source_target_pairs={{1,0},{2,1},{3,2},{4,3},{5,4},{6,5},{7,6},{8,7},{9,8},{10,9},{11,1... | collective-permute-start | bytes 49160 | tf_op jit(solution)/shard_map/ppermute | solution.py:13
  523.4 435.1 %all-gather.12.cloned.1.call-start = ((), (), s32[]{:S(2)}) async-start(), calls=%async_computation.3 | async-start | bytes 3342336 | tf_op jit(solution)/shard_map/all_gather | solution.py:79
  535.1 39.2 %collective-permute-start.24 = (bf16[64,128]{1,0:T(8,128)(2,1)S(1)}, bf16[64,128]{1,0:T(8,128)(2,1)S(1)}, u32[]{:S(2)}, u32[]{:S(2)}) collective-permute-start(bf16[64,128]{1,0:T(8,128)(2,1)S(1)} %bitcast.470), channel_id=1, source_target_pairs={{0,16},{16,32},{32,48},{48,64},{64,80},{80,96},{96,112},{112,128},... | collective-permute-start | bytes 49160 | tf_op jit(solution)/shard_map/ppermute | solution.py:13
  578.3 36.9 %collective-permute-start.33 = (bf16[64,128]{1,0:T(8,128)(2,1)S(1)}, bf16[64,128]{1,0:T(8,128)(2,1)S(1)}, u32[]{:S(2)}, u32[]{:S(2)}) collective-permute-start(bf16[64,128]{1,0:T(8,128)(2,1)S(1)} %bitcast.421), channel_id=1, source_target_pairs={{16,0},{32,16},{48,32},{64,48},{80,64},{96,80},{112,96},{128,112},... | collective-permute-start | bytes 49160 | tf_op jit(solution)/shard_map/ppermute | solution.py:13
  580.2 35.6 %collective-permute-start.25 = (bf16[64,128]{1,0:T(8,128)(2,1)S(1)}, bf16[64,128]{1,0:T(8,128)(2,1)S(1)}, u32[]{:S(2)}, u32[]{:S(2)}) collective-permute-start(bf16[64,128]{1,0:T(8,128)(2,1)S(1)} %collective-permute-done.24), channel_id=1, source_target_pairs={{0,1},{1,2},{2,3},{3,4},{4,5},{5,6},{6,7},{7,8},{8,9},{9,10},{10,1... | collective-permute-start | bytes 49160 | tf_op jit(solution)/shard_map/ppermute | solution.py:13
  582.1 34.3 %collective-permute-start.28 = (bf16[64,128]{1,0:T(8,128)(2,1)S(1)}, bf16[64,128]{1,0:T(8,128)(2,1)S(1)}, u32[]{:S(2)}, u32[]{:S(2)}) collective-permute-start(bf16[64,128]{1,0:T(8,128)(2,1)S(1)} %collective-permute-done.27), channel_id=1, source_target_pairs={{1,0},{2,1},{3,2},{4,3},{5,4},{6,5},{7,6},{8,7},{9,8},{10,9},{11,1... | collective-permute-start | bytes 49160 | tf_op jit(solution)/shard_map/ppermute | solution.py:13
  741.0 349.0 %all-gather.14.cloned.1.call-start = ((), (), s32[]{:S(2)}) async-start(), calls=%async_computation.4 | async-start | bytes 3342336 | tf_op jit(solution)/shard_map/all_gather | solution.py:79
  752.8 39.2 %collective-permute-start.36 = (bf16[64,128]{1,0:T(8,128)(2,1)S(1)}, bf16[64,128]{1,0:T(8,128)(2,1)S(1)}, u32[]{:S(2)}, u32[]{:S(2)}) collective-permute-start(bf16[64,128]{1,0:T(8,128)(2,1)S(1)} %bitcast.471), channel_id=1, source_target_pairs={{0,16},{16,32},{32,48},{48,64},{64,80},{80,96},{96,112},{112,128},... | collective-permute-start | bytes 49160 | tf_op jit(solution)/shard_map/ppermute | solution.py:13
  795.9 36.7 %collective-permute-start.45 = (bf16[64,128]{1,0:T(8,128)(2,1)S(1)}, bf16[64,128]{1,0:T(8,128)(2,1)S(1)}, u32[]{:S(2)}, u32[]{:S(2)}) collective-permute-start(bf16[64,128]{1,0:T(8,128)(2,1)S(1)} %bitcast.422), channel_id=1, source_target_pairs={{16,0},{32,16},{48,32},{64,48},{80,64},{96,80},{112,96},{128,112},... | collective-permute-start | bytes 49160 | tf_op jit(solution)/shard_map/ppermute | solution.py:13
  797.9 35.4 %collective-permute-start.37 = (bf16[64,128]{1,0:T(8,128)(2,1)S(1)}, bf16[64,128]{1,0:T(8,128)(2,1)S(1)}, u32[]{:S(2)}, u32[]{:S(2)}) collective-permute-start(bf16[64,128]{1,0:T(8,128)(2,1)S(1)} %collective-permute-done.36), channel_id=1, source_target_pairs={{0,1},{1,2},{2,3},{3,4},{4,5},{5,6},{6,7},{7,8},{8,9},{9,10},{10,1... | collective-permute-start | bytes 49160 | tf_op jit(solution)/shard_map/ppermute | solution.py:13
  799.8 34.1 %collective-permute-start.40 = (bf16[64,128]{1,0:T(8,128)(2,1)S(1)}, bf16[64,128]{1,0:T(8,128)(2,1)S(1)}, u32[]{:S(2)}, u32[]{:S(2)}) collective-permute-start(bf16[64,128]{1,0:T(8,128)(2,1)S(1)} %collective-permute-done.39), channel_id=1, source_target_pairs={{1,0},{2,1},{3,2},{4,3},{5,4},{6,5},{7,6},{8,7},{9,8},{10,9},{11,1... | collective-permute-start | bytes 49160 | tf_op jit(solution)/shard_map/ppermute | solution.py:13
  1134.2 40.2 %collective-permute-start.57 = (bf16[64,128]{1,0:T(8,128)(2,1)}, bf16[64,128]{1,0:T(8,128)(2,1)}, u32[]{:S(2)}, u32[]{:S(2)}) collective-permute-start(bf16[64,128]{1,0:T(8,128)(2,1)} %bitcast.355), channel_id=1, source_target_pairs={{16,0},{32,16},{48,32},{64,48},{80,64},{96,80},{112,96},{128,112},... | collective-permute-start | bytes 49160 | tf_op jit(solution)/shard_map/ppermute | solution.py:13
  1136.7 39.1 %collective-permute-start.49 = (bf16[64,128]{1,0:T(8,128)(2,1)}, bf16[64,128]{1,0:T(8,128)(2,1)}, u32[]{:S(2)}, u32[]{:S(2)}) collective-permute-start(bf16[64,128]{1,0:T(8,128)(2,1)} %collective-permute-done.48), channel_id=1, source_target_pairs={{0,1},{1,2},{2,3},{3,4},{4,5},{5,6},{6,7},{7,8},{8,9},{9,10},{10,1... | collective-permute-start | bytes 49160 | tf_op jit(solution)/shard_map/ppermute | solution.py:13
  1138.6 38.5 %collective-permute-start.52 = (bf16[64,128]{1,0:T(8,128)(2,1)}, bf16[64,128]{1,0:T(8,128)(2,1)}, u32[]{:S(2)}, u32[]{:S(2)}) collective-permute-start(bf16[64,128]{1,0:T(8,128)(2,1)} %collective-permute-done.51), channel_id=1, source_target_pairs={{1,0},{2,1},{3,2},{4,3},{5,4},{6,5},{7,6},{8,7},{9,8},{10,9},{11,1... | collective-permute-start | bytes 49160 | tf_op jit(solution)/shard_map/ppermute | solution.py:13
  (64 other events, 2003.7 us)
Sparse Core Ops, SparseCore 0:
  96.2 134.4 all-gather.5
  306.0 131.6 all-gather.7
  523.5 131.7 all-gather.9
  741.1 131.7 all-gather.11
  958.6 131.3 all-gather.13
